TPU v7x, 128 devices: a whole 4x4x4 slice. The times are simulated.
128 devices in a mesh: row: 64 (over z, y, x), col: 2 (over core).
Axes of the slice: x: 4, y: 4, z: 4, core: 2. Of those that a mesh axis runs over, the one named last changes fastest.
Arguments:
- rhs: float32 [2, 64, 1024, 1024], P(None, 'row', None, 'col'), may hold values from -8 to 8
- panels: float32 [2, 2, 64, 1024, 1024], P(None, None, 'row', None, 'col'), may hold values from -0.1875 to 0.1875
- inverses: float32 [2, 1024, 1024], replicated, may hold values from -1 to 4, as said below
Outputs:
- result: float32 [2, 64, 1024, 1024], P(None, 'row', None, 'col')
Inputs may be any that keep to these rules, and one draw needn't show every extreme that they name: Each inverses[k] is lower triangular with a positive diagonal.
All inputs are finite; a program needn't handle non-finite values.
Results may differ from a plain program's by a relative error of at most 0.000075.
Values sent between devices are 32-bit elements; how exact they have to be, the bound alone decides.
No kernel may reach another device: no remote copies, remote signals or barrier semaphores. Data moves between devices by JAX's collectives and lax.ppermute only.
A program may use at most 128 MiB of HBM per device.

v0:
```python
import jax
import jax.numpy as jnp
from jax import lax
from jax.sharding import PartitionSpec as P


def broadcast(value, axis, source):
    kept = jnp.where(lax.axis_index(axis) == source, value, 0).astype(value.dtype)
    return lax.psum(kept, axis)


def per_device(rhs, panels, inverses):
    highest = lax.Precision.HIGHEST
    row_index = lax.axis_index("row")
    row_count = lax.axis_size("row")
    slot_count = rhs.shape[0]
    block_ids = (jnp.arange(slot_count, dtype=jnp.int32) * row_count + row_index)[
        :, None, None, None
    ]

    def solve_block(current, panel_index):
        owner_value = jnp.dot(
            inverses[panel_index], current, precision=highest, preferred_element_type=jnp.float32
        )
        solved = broadcast(owner_value, "row", panel_index)
        return (solved, solved)

    def apply_panel(tiles, solved):
        return jnp.einsum(
            "sqin,nr->sqir",
            lax.all_gather(tiles, "col", axis=3, tiled=True),
            solved,
            precision=highest,
            preferred_element_type=jnp.float32,
        )

    solved0, spread0 = solve_block(rhs[0, 0], 0)
    sectioned = rhs - apply_panel(panels[0], solved0)
    sectioned = jnp.where(block_ids >= 1, sectioned, solved0)
    solved1, spread1 = solve_block(sectioned[0, 0], 1)
    updated = sectioned - apply_panel(panels[1], solved1)
    return jnp.where(block_ids >= 2, updated, jnp.where(block_ids == 1, solved1, sectioned))


def solution(mesh):
    placed = (P(None, "row", None, "col"), P(None, None, "row", None, "col"), P())
    return jax.shard_map(
        per_device,
        mesh=mesh,
        in_specs=placed,
        out_specs=P(None, "row", None, "col"),
        check_vma=False,
    )
```

profile of v0, /device:TPU:1, one launch (start us, length us, event | category | flops | bytes accessed | tf_op | source)
XLA Modules:
  0.0 356.4 jit_solution(1099905670875541732)
XLA Ops:
  7.4 0.0 all-reduce.3.cloned.1.call-start
  7.4 10.3 %fusion.20 = f32[1024,512]{1,0:T(8,128)} fusion(f32[2,1,1024,512]{3,2,1,0:T(8,128)} %param.3, f32[2,1024,1024]{2,1,0:T(8,128)} %param.5, pred[]{:T(512)S(6)} %eq.14), kind=kOutput, calls=%fused_computation.20 | convolution fusion | flops 6442975232 | bytes 8388609 | tf_op jit(solution)/shard_map/dot_general | solution.py:22
  17.6 0.0 all-reduce.3.cloned.1.call-update
  17.7 0.0 all-gather.5.cloned.1.call-start
  17.7 7.7 %fusion.27 = (f32[1,2,1,1024,512]{4,3,1,2,0:T(8,128)}, f32[1,2,1,1024,512]{4,3,1,2,0:T(8,128)}) fusion(f32[2,2,1,1024,512]{4,3,1,2,0:T(8,128)} %bitcast.52), kind=kLoop, calls=%fused_computation.25 | loop fusion | bytes 16777216 | tf_op jit(solution)/shard_map/slice | solution.py:41
  25.4 0.0 all-gather.5.cloned.1.call-update
  25.4 0.0 all-gather.7.cloned.1.call-start
  25.5 0.5 all-gather.7.cloned.1.call-update
  26.0 0.0 all-reduce.5.cloned.1.call-start
  26.1 5.4 %copy.6 = f32[2,1,1024,512]{2,3,0,1:T(8,128)} copy(f32[2,1,1024,512]{3,2,1,0:T(8,128)} %param.3) | data formatting | bytes 8388608 | tf_op args[0]
  31.5 120.0 %all-reduce.3.cloned.1.call-done = f32[1024,512]{1,0:T(8,128)} async-done(((f32[1024,512]{1,0:T(8,128)}), f32[1024,512]{1,0:T(8,128)}) %all-reduce.3.cloned.1.call-update) | async-done | bytes 2097168 | tf_op jit(solution)/shard_map/psum | solution.py:9
  151.5 1.9 copy.7
  153.4 0.0 all-gather.5.cloned.1.call-done
  153.4 30.6 %fusion.5 = f32[2,1,1024,512]{2,3,0,1:T(8,128)S(1)} fusion(f32[2,1,1024,512]{2,3,0,1:T(8,128)} %copy.6, f32[1,2,1,1024,1024]{4,3,1,2,0:T(8,128)} %all-gather.5.cloned.1.call-done, f32[1024,512]{1,0:T(8,128)} %all-reduce.3.cloned.1.call-done, f32[1024,512]{0,1:T(8,128)S(1)} %copy.7, pred[2]{0:T(512)(128)(4,1)S(1)} %broadcast_compare_fusion.1), kind=kOutput, calls=%fused_computation.7 | convolution fusion | flops 12886999040 | bytes 20971522 | tf_op jit(solution)/shard_map/sqin,nr->sqir/dot_general | solution.py:29
  184.0 0.0 copy-start
  184.0 2.0 copy-done
  186.0 9.6 %select_bitcast_fusion = f32[1024,512]{0,1:T(8,128)} fusion(f32[2,1024,1024]{2,1,0:T(8,128)} %param.5, f32[2,1,1024,512]{2,3,0,1:T(8,128)S(1)} %fusion.5, pred[]{:T(512)S(6)} %eq.15), kind=kOutput, calls=%fused_computation.18 | convolution fusion | flops 6442975232 | bytes 8388609 | tf_op jit(solution)/shard_map/dot_general | solution.py:22
  195.7 0.0 all-reduce.5.cloned.1.call-update
  195.7 0.0 all-gather.7.cloned.1.call-done
  195.8 129.9 %all-reduce.5.cloned.1.call-done = f32[1024,512]{0,1:T(8,128)} async-done(((f32[1024,512]{0,1:T(8,128)}), f32[1024,512]{0,1:T(8,128)}) %all-reduce.5.cloned.1.call-update) | async-done | bytes 2097168 | tf_op jit(solution)/shard_map/psum | solution.py:9
  325.7 18.0 %fusion.4 = f32[2,1,1024,512]{2,3,0,1:T(8,128)} fusion(f32[2,1,1024,512]{2,3,0,1:T(8,128)} %copy-done, f32[1,2,1,1024,1024]{4,3,1,2,0:T(8,128)} %all-gather.7.cloned.1.call-done, f32[1024,512]{0,1:T(8,128)} %all-reduce.5.cloned.1.call-done, pred[2]{0:T(512)(128)(4,1)S(1)} %get-tuple-element.7, pred[2]{0:T(512)(128)(4,1)S(1)} %get-tuple-element.8), kind=kOutput, calls=%fused_computation.5 | convolution fusion | flops 12888047616 | bytes 18874372 | tf_op jit(solution)/shard_map/sqin,nr->sqir/dot_general | solution.py:29
  343.6 5.4 %copy.9 = f32[2,1,1024,512]{3,2,1,0:T(8,128)} copy(f32[2,1,1024,512]{2,3,0,1:T(8,128)} %fusion.4) | data formatting | bytes 8388608 | tf_op jit(solution)/shard_map/jit(_where)/select_n | solution.py:42
  (2 shorter events, 0.0 us)
Async XLA Ops:
  7.4 144.1 %all-reduce.3.cloned.1.call-start = ((), (), s32[]{:S(2)}) async-start(), calls=%async_computation | async-start | bytes 4194304 | tf_op jit(solution)/shard_map/psum | solution.py:9
  17.7 135.8 %all-gather.5.cloned.1.call-start = ((), (), s32[]{:S(2)}) async-start(), calls=%async_computation.2 | async-start | bytes 12582912 | tf_op jit(solution)/shard_map/all_gather | solution.py:31
  25.4 170.3 %all-gather.7.cloned.1.call-start = ((), (), s32[]{:S(2)}) async-start(), calls=%async_computation.3 | async-start | bytes 12582912 | tf_op jit(solution)/shard_map/all_gather | solution.py:31
  26.0 299.7 %all-reduce.5.cloned.1.call-start = ((), (), s32[]{:S(2)}) async-start(), calls=%async_computation.1 | async-start | bytes 4194304 | tf_op jit(solution)/shard_map/psum | solution.py:9
  184.0 2.0 copy-start
Sparse Core Ops, SparseCore 0:
  17.8 133.6 all-reduce.2
  195.8 129.8 all-reduce.4
Sparse Core Ops, SparseCore 1:
  25.5 26.1 all-gather.4
  53.1 23.8 all-gather.6
where the time goes:
time: 358 us; the launch traced here: 356 us
  waiting for transfers between devices  251 us (70%)
  matrix products  68.5 us (19%)
  local copies, waits for them, and re-layouts  22.4 us (6%)
  between operations  14.9 us (4%)
    psum x2, waiting for transfers between devices, broadcast(): return lax.psum(kept, axis)  250 us
    dot_general x2, matrix products, apply_panel(): jnp.einsum('sqin,nr->sqir', lax.all_gather(tiles, 'col', axis=3, tiled=Tr...  48.5 us
    dot_general x2, matrix products, solve_block(): jnp.dot(inverses[panel_index], current, precision=highest, preferred_elem...  19.9 us
    slice x1, local copies, waits for them, and re-layouts, per_device(): updated = sectioned - apply_panel(panels[1], solved1)  7.67 us
    unnamed x3, local copies, waits for them, and re-layouts  7.42 us
  transfers between devices with their start and end apart: 4, of which 2 were waited for; matrix products, arithmetic and copies ran while one was open for 16% of the time, Pallas kernels for 0%

commit v1 on v0

v1 whole, which is shorter than its diff:
```python
import jax
import jax.numpy as jnp
from jax import lax
from jax.sharding import PartitionSpec as P


def per_device(rhs, panels, inverses):
    highest = lax.Precision.HIGHEST
    row_index = lax.axis_index("row")
    row_count = lax.axis_size("row")
    slot_count = rhs.shape[0]
    block_ids = (jnp.arange(slot_count, dtype=jnp.int32) * row_count + row_index)[
        :, None, None, None
    ]

    def dot(a, b):
        return jnp.dot(a, b, precision=highest, preferred_element_type=jnp.float32)

    wanted = jnp.stack([rhs[0, 0], rhs[0, 0], panels[0, 0, 0]])
    owner = jnp.array([0, 1, 1], dtype=jnp.int32)[:, None, None]
    spread = lax.psum(jnp.where(owner == row_index, wanted, 0).astype(wanted.dtype), "row")
    rhs0, rhs1, tile_half = spread[0], spread[1], spread[2]

    def apply_panel(tiles, solved):
        return jnp.einsum(
            "sqin,nr->sqir",
            lax.all_gather(tiles, "col", axis=3, tiled=True),
            solved,
            precision=highest,
            preferred_element_type=jnp.float32,
        )

    solved0 = dot(inverses[0], rhs0)
    sectioned = rhs - apply_panel(panels[0], solved0)
    sectioned = jnp.where(block_ids >= 1, sectioned, solved0)
    tile = lax.all_gather(tile_half, "col", axis=1, tiled=True)
    solved1 = dot(inverses[1], rhs1 - dot(tile, solved0))
    updated = sectioned - apply_panel(panels[1], solved1)
    return jnp.where(block_ids >= 2, updated, jnp.where(block_ids == 1, solved1, sectioned))


def solution(mesh):
    placed = (P(None, "row", None, "col"), P(None, None, "row", None, "col"), P())
    return jax.shard_map(
        per_device,
        mesh=mesh,
        in_specs=placed,
        out_specs=P(None, "row", None, "col"),
        check_vma=False,
    )
```

time: 358 us -> 273 us (0.76)
  waiting for transfers between devices: 251 us -> 151 us
  matrix products: 68.5 us -> 79.1 us
    psum x2 -> x1, waiting for transfers between devices: 250 us -> 151 us  [per_device(): lax.psum(jnp.where(owner == row_index, wanted, 0).astype(wanted.dtype), '...]
    dot_general x2 -> x3, matrix products: 19.9 us -> 42 us  [dot(): return jnp.dot(a, b, precision=highest, preferred_element_type=jnp.float32)]
    dot_general x2, matrix products: 48.5 us -> 37.1 us  [apply_panel(): jnp.einsum('sqin,nr->sqir', lax.all_gather(tiles, 'col', axis=3, tiled=Tr...]
    slice x1 -> x2, local copies, waits for them, and re-layouts: 7.67 us -> 11 us  [the longest x1 7.87 us: per_device(): sectioned = rhs - apply_panel(panels[0], solved0)]
    unnamed x3 -> x5, local copies, waits for them, and re-layouts: 7.42 us -> 6.66 us
  transfers between devices with their start and end apart: 4 -> 4, of which waited for: 2 -> 1; matrix products, arithmetic and copies ran while one was open for 16% -> 27% of each run, Pallas kernels for 0% -> 0%
where the time goes in v1:
time: 273 us; the launch traced here: 272 us
  waiting for transfers between devices  151 us (55%)
  matrix products  79.1 us (29%)
  local copies, waits for them, and re-layouts  25.1 us (9%)
  between operations  13.2 us (5%)
  other arithmetic  3.59 us (1%)
    psum x1, waiting for transfers between devices, per_device(): lax.psum(jnp.where(owner == row_index, wanted, 0).astype(wanted.dtype), '...  151 us
    dot_general x3, matrix products, dot(): return jnp.dot(a, b, precision=highest, preferred_element_type=jnp.float32)  42 us
    dot_general x2, matrix products, apply_panel(): jnp.einsum('sqin,nr->sqir', lax.all_gather(tiles, 'col', axis=3, tiled=Tr...  37.1 us
    slice x1, local copies, waits for them, and re-layouts, per_device(): sectioned = rhs - apply_panel(panels[0], solved0)  7.87 us
    unnamed x5, local copies, waits for them, and re-layouts  6.66 us
  transfers between devices with their start and end apart: 4, of which 1 were waited for; matrix products, arithmetic and copies ran while one was open for 27% of the time, Pallas kernels for 0%

profile of v1, /device:TPU:1, one launch (start us, length us, event | category | flops | bytes accessed | tf_op | source)
XLA Modules:
  0.0 272.3 jit_solution(185476620764520095)
XLA Ops:
  6.5 0.0 all-reduce.2.cloned.1.call-start
  6.5 0.0 copy-start
  6.5 0.0 copy-start.1
  6.5 1.9 slice_bitcast_fusion.3
  8.5 0.9 copy-done
  9.4 0.2 slice_bitcast_fusion.4
  9.5 0.0 copy-done.1
  9.6 3.6 %maximum_select_fusion = f32[3,1024,512]{2,1,0:T(8,128)} fusion(f32[1,1024,512]{2,1,0:T(8,128)S(1)} %slice_bitcast_fusion.3, f32[1,1024,512]{2,1,0:T(8,128)S(1)} %slice_bitcast_fusion.4, pred[3]{0:T(512)(128)(4,1)S(1)} %broadcast_compare_fusion), kind=kLoop, calls=%fused_computation.4 | loop fusion | flops 4718592 | bytes 10485763 | tf_op jit(solution)/shard_map/jit(_where)/select_n | solution.py:21
  13.1 0.0 all-reduce.2.cloned.1.call-update
  13.1 0.0 all-gather.9.cloned.1.call-start
  13.2 150.6 %all-reduce.2.cloned.1.call-done = f32[3,1024,512]{2,1,0:T(8,128)} async-done(((f32[3,1024,512]{2,1,0:T(8,128)}), f32[3,1024,512]{2,1,0:T(8,128)}) %all-reduce.2.cloned.1.call-update) | async-done | bytes 6291472 | tf_op jit(solution)/shard_map/psum | solution.py:21
  163.8 3.1 %slice.40 = f32[1,1024,512]{2,1,0:T(8,128)} slice(f32[3,1024,512]{2,1,0:T(8,128)} %all-reduce.2.cloned.1.call-done), slice={[2:3], [0:1024], [0:512]} | slice | bytes 4194304 | tf_op jit(solution)/shard_map/slice | solution.py:22
  166.9 0.0 all-gather.9.cloned.1.call-update
  166.9 0.0 all-gather.11.cloned.1.call-start
  167.0 7.9 %fusion.20 = (f32[1,2,1,1024,512]{4,3,1,2,0:T(8,128)}, f32[1,2,1,1024,512]{4,3,1,2,0:T(8,128)}) fusion(f32[2,2,1,1024,512]{4,3,1,2,0:T(8,128)} %bitcast.56), kind=kLoop, calls=%fused_computation.29 | loop fusion | bytes 16777216 | tf_op jit(solution)/shard_map/slice | solution.py:34
  174.9 0.0 all-gather.11.cloned.1.call-update
  174.9 0.2 all-gather.7.cloned.1.call-start
  175.1 0.3 all-gather.7.cloned.1.call-update
  175.5 5.8 %copy.6 = f32[2,1,1024,512]{2,3,0,1:T(8,128)} copy(f32[2,1,1024,512]{3,2,1,0:T(8,128)} %param.4) | data formatting | bytes 8388608 | tf_op args[0]
  181.3 15.9 %fusion.10 = f32[512,1024]{1,0:T(8,128)S(1)} fusion(f32[2,1024,1024]{2,1,0:T(8,128)} %param.6, f32[3,1024,512]{2,1,0:T(8,128)} %all-reduce.2.cloned.1.call-done), kind=kOutput, calls=%fused_computation.13 | convolution fusion | flops 6442450944 | bytes 8388608 | tf_op jit(solution)/shard_map/dot_general | solution.py:17
  197.1 0.0 all-gather.9.cloned.1.call-done
  197.2 9.0 %fusion.8 = f32[1024,512]{1,0:T(8,128)S(1)} fusion(f32[512,1024]{1,0:T(8,128)S(1)} %fusion.10, f32[1,1024,1024]{2,1,0:T(8,128)} %all-gather.9.cloned.1.call-done), kind=kOutput, calls=%fused_computation.11 | convolution fusion | flops 6442450944 | bytes 8388608 | tf_op jit(solution)/shard_map/dot_general | solution.py:17
  206.2 17.0 %fusion.6 = f32[512,1024]{1,0:T(8,128)} fusion(f32[2,1024,1024]{2,1,0:T(8,128)} %param.6, f32[1024,512]{1,0:T(8,128)S(1)} %fusion.8, f32[3,1024,512]{2,1,0:T(8,128)} %all-reduce.2.cloned.1.call-done), kind=kOutput, calls=%fused_computation.9 | convolution fusion | flops 6442975232 | bytes 10485760 | tf_op jit(solution)/shard_map/dot_general | solution.py:17
  223.3 0.0 all-gather.11.cloned.1.call-done
  223.3 19.1 %fusion = f32[512,2,1024]{2,0,1:T(8,128)} fusion(f32[1,2,1,1024,1024]{4,3,1,2,0:T(8,128)} %all-gather.11.cloned.1.call-done, f32[512,1024]{1,0:T(8,128)} %fusion.6), kind=kOutput, calls=%fused_computation | convolution fusion | flops 12884901888 | bytes 14680064 | tf_op jit(solution)/shard_map/sqin,nr->sqir/dot_general | solution.py:25
  242.4 0.0 all-gather.7.cloned.1.call-done
  242.4 18.0 %fusion.4 = f32[2,1,1024,512]{2,3,0,1:T(8,128)} fusion(f32[512,2,1024]{2,0,1:T(8,128)} %fusion, f32[2,1,1024,512]{2,3,0,1:T(8,128)} %copy.6, f32[1,2,1,1024,1024]{4,3,1,2,0:T(8,128)} %all-gather.7.cloned.1.call-done, f32[512,1024]{1,0:T(8,128)S(1)} %fusion.10, f32[1024,512]{0,1:T(8,128)} %bitcast.55, f32[1024,512]{0,1:T(8,128)S(1)} %bitcast.54, ...), kind=kOutput, calls=%fused_computation.6 | convolution fusion | flops 12890144768 | bytes 27262982 | tf_op jit(solution)/shard_map/sqin,nr->sqir/dot_general | solution.py:25
  260.4 5.4 %copy.8 = f32[2,1,1024,512]{3,2,1,0:T(8,128)} copy(f32[2,1,1024,512]{2,3,0,1:T(8,128)} %fusion.4) | data formatting | bytes 8388608 | tf_op jit(solution)/shard_map/jit(_where)/select_n | solution.py:39
  (3 shorter events, 0.0 us)
Async XLA Ops:
  6.5 157.2 %all-reduce.2.cloned.1.call-start = ((), (), s32[]{:S(2)}) async-start(), calls=%async_computation | async-start | bytes 12582912 | tf_op jit(solution)/shard_map/psum | solution.py:21
  6.5 2.8 %copy-start = (f32[2,1,1024,512]{3,2,1,0:T(8,128)S(1)}, f32[2,1,1024,512]{3,2,1,0:T(8,128)}, u32[]{:S(2)}) copy-start(f32[2,1,1024,512]{3,2,1,0:T(8,128)} %param.4) | copy-start | bytes 12582916
  6.5 3.0 %copy-start.1 = (s32[3]{0:T(128)S(1)}, s32[3]{0:T(128)}, u32[]{:S(2)}) copy-start(s32[3]{0:T(128)} %constant.17.clone) | copy-start | bytes 40
  13.1 184.0 %all-gather.9.cloned.1.call-start = ((), (), s32[]{:S(2)}) async-start(), calls=%async_computation.2 | async-start | bytes 6291456 | tf_op jit(solution)/shard_map/all_gather | solution.py:36
  166.9 56.3 %all-gather.11.cloned.1.call-start = ((), (), s32[]{:S(2)}) async-start(), calls=%async_computation.3 | async-start | bytes 12582912 | tf_op jit(solution)/shard_map/all_gather | solution.py:27
  174.9 67.5 %all-gather.7.cloned.1.call-start = ((), (), s32[]{:S(2)}) async-start(), calls=%async_computation.1 | async-start | bytes 12582912 | tf_op jit(solution)/shard_map/all_gather | solution.py:27
Sparse Core Ops, SparseCore 0:
  13.3 150.4 all-reduce.1
  167.1 16.8 all-gather.8
  185.6 23.8 all-gather.10
  211.1 23.8 all-gather.6
